TPU v7x, 256 devices: a whole 4x4x8 slice. The times are simulated.
256 devices in a mesh: row: 16 (over z_lo, x, core), col: 16 (over z_hi, y).
Axes of the slice: x: 4, y: 4, z: 8 (z_hi: 4, z_lo: 2; z = z_hi * 2 + z_lo), core: 2. Of those that a mesh axis runs over, the one named last changes fastest.
Arguments:
- features: bfloat16 [65536, 512], P(('col', 'row')), may hold values from -6 to 6
- weight: bfloat16 [512, 512], replicated, may hold values from -0.25 to 0.25
- entry_values: bfloat16 [16, 16, 32, 128, 128], P('row', 'col'), may hold values from 0.0009994507 to 0.019897461
- block_rows: int32 [16, 16, 32], P('row', 'col'), may hold values from 0 to 31
- block_cols: int32 [16, 16, 32], P('row', 'col'), may hold values from 0 to 31
- entry_counts: int32 [16, 16], P('row', 'col'), may hold values from 8 to 32, as said below
- cotangent: bfloat16 [65536, 512], P(('row', 'col')), may hold values from -1.5 to 1.5
Outputs:
- output: bfloat16 [65536, 512], P(('row', 'col'))
- grad_features: bfloat16 [65536, 512], P(('col', 'row'))
- grad_weight: float32 [512, 512], replicated
Inputs may be any that keep to these rules, and one draw needn't show every extreme that they name: `entry_counts`: each grid cell has at least 8 live slots; at least one cell has all 32 live.
All inputs are finite; a program needn't handle non-finite values.
Results may differ from a plain program's by a relative error of at most 0.022.
Values may be sent and summed in bfloat16 or wider, within the bound.
No kernel may reach another device: no remote copies, remote signals or barrier semaphores. Data moves between devices by JAX's collectives and lax.ppermute only.
A program may use at most 128 MiB of HBM per device.

v0:
```python
import jax
import jax.numpy as jnp
from jax import lax
from jax.sharding import PartitionSpec as P


def block_terms(values, source_ids, target_ids, live_count, source, target_blocks, transpose):
    entry_total = values.shape[0]
    block_side = values.shape[1]
    feature_count = source.shape[1]
    group_size = min(32, entry_total)
    source_tiles = source.reshape(-1, block_side, feature_count)

    def one_group(group_index, running):
        first_entry = group_index * group_size
        tiles = jnp.take(source_tiles, source_ids, axis=0)
        if transpose:
            products = jnp.einsum("kba,kbf->kaf", values, tiles, preferred_element_type=jnp.float32)
        else:
            products = jnp.einsum("kab,kbf->kaf", values, tiles, preferred_element_type=jnp.float32)
        alive_mask = (first_entry + jnp.arange(group_size) < live_count).astype(jnp.float32)
        return running.at[target_ids].add(products * alive_mask[:, None, None])

    zero_sum = jnp.zeros((target_blocks, block_side, feature_count), jnp.float32)
    trip_count = entry_total // group_size
    running = lax.fori_loop(0, trip_count, one_group, zero_sum)
    return running.reshape(target_blocks * block_side, feature_count)


def silu_slope(summed):
    sigmoid_value = jax.nn.sigmoid(summed)
    return sigmoid_value * (1.0 + summed * (1.0 - sigmoid_value))


def shards(features, weight, entry_values, block_rows, block_cols, entry_counts, cotangent):
    values = entry_values[0, 0]
    row_ids = block_rows[0, 0]
    col_ids = block_cols[0, 0]
    live_count = entry_counts[0, 0]
    local_rows = features.shape[0]
    block_side = values.shape[1]
    row_span = lax.axis_size("col") * local_rows
    col_span = lax.axis_size("row") * local_rows
    projected = jnp.dot(features, weight, preferred_element_type=jnp.float32).astype(jnp.bfloat16)
    panel = lax.all_gather(projected, "row", axis=0, tiled=True)
    forward_terms = block_terms(
        values, col_ids, row_ids, live_count, panel, row_span // block_side, False
    )
    own_sum = lax.psum_scatter(
        forward_terms.astype(jnp.bfloat16), "col", scatter_dimension=0, tiled=True
    ).astype(jnp.float32)
    output = jax.nn.silu(own_sum).astype(jnp.bfloat16)
    own_upstream = (cotangent.astype(jnp.float32) * silu_slope(own_sum)).astype(jnp.bfloat16)
    upstream = lax.all_gather(own_upstream, "col", axis=0, tiled=True)
    backward_terms = block_terms(
        values, row_ids, col_ids, live_count, upstream, col_span // block_side, True
    )
    grad_projected = lax.psum_scatter(
        backward_terms.astype(jnp.bfloat16), "row", scatter_dimension=0, tiled=True
    )
    weight_term = lax.dot_general(
        features, grad_projected, (((0,), (0,)), ((), ())), preferred_element_type=jnp.float32
    )
    weight_part = lax.psum_scatter(weight_term, "row", scatter_dimension=0, tiled=True)
    weight_part = lax.psum(weight_part, "col")
    grad_weight = lax.all_gather(weight_part, "row", axis=0, tiled=True)
    grad_features = lax.dot_general(
        grad_projected, weight, (((1,), (1,)), ((), ())), preferred_element_type=jnp.float32
    ).astype(jnp.bfloat16)
    return (output, grad_features, grad_weight)


def solution(mesh):
    placed = (
        P(("col", "row"), None),
        P(),
        P("row", "col", None, None, None),
        P("row", "col", None),
        P("row", "col", None),
        P("row", "col"),
        P(("row", "col"), None),
    )
    return jax.shard_map(
        shards,
        mesh=mesh,
        in_specs=placed,
        out_specs=(P(("row", "col"), None), P(("col", "row"), None), P()),
        check_vma=False,
    )
```

profile of v0, /device:TPU:1, one launch (start us, length us, event | category | flops | bytes accessed | tf_op | source)
XLA Modules:
  0.0 675.2 jit_solution(13709387366234247826)
XLA Ops:
  7.2 2.2 convolution_convert_fusion.1
  12.1 42.2 %all-gather.4.cloned.1.call-done = bf16[4096,512]{1,0:T(8,128)(2,1)} async-done(((bf16[256,512]{1,0:T(8,128)(2,1)}), bf16[4096,512]{1,0:T(8,128)(2,1)}) %all-gather.4.cloned.1.call-update) | async-done | bytes 4194320 | tf_op jit(solution)/shard_map/all_gather | solution.py:45
  54.4 4.9 gather_fusion
  59.3 7.1 %multiply_bitcast_fusion.1 = f32[32,128,512]{1,2,0:T(8,128)} fusion(f32[32]{0:T(128)S(1)} %get-tuple-element.53, bf16[32,128,512]{2,1,0:T(8,128)(2,1)} %gather_fusion, pred[32]{0:T(512)(128)(4,1)S(1)} %get-tuple-element.52, bf16[1,1,32,128,128]{4,3,2,1,0:T(8,128)(2,1)S(1)} %copy-done), kind=kOutput, calls=%fused_computation.5 | convolution fusion | flops 541065216 | bytes 13631648 | tf_op jit(solution)/shard_map/while/body/eval_jaxpr/kab,kbf->kaf/dot_general | solution.py:20
  66.5 9.0 %copy.19 = f32[32,128,512]{2,1,0:T(8,128)} copy(f32[32,128,512]{1,2,0:T(8,128)} %multiply_bitcast_fusion.1) | data formatting | bytes 16777216 | tf_op jit(solution)/shard_map/while/body/eval_jaxpr/mul | solution.py:22
  75.5 4.3 broadcast.55.clone
  79.8 18.5 %scatter_fusion = f32[32,128,512]{2,1,0:T(8,128)} fusion(f32[32,128,512]{2,1,0:T(8,128)} %broadcast.55.clone, s32[32]{0:T(128)S(1)} %fusion.22, f32[32,128,512]{2,1,0:T(8,128)} %copy.19), kind=kCustom, calls=%fused_computation.2 | custom fusion | flops 2097152 | bytes 25165952 | tf_op jit(solution)/shard_map/while/body/eval_jaxpr/scatter-add | solution.py:22
  98.3 6.0 convert_element_type.42
  104.3 95.2 %reduce-scatter.6.cloned.1.call-done = bf16[256,512]{1,0:T(8,128)(2,1)} async-done(((bf16[4096,512]{1,0:T(8,128)(2,1)}), bf16[256,512]{1,0:T(8,128)(2,1)}) %reduce-scatter.6.cloned.1.call-update) | async-done | bytes 262160 | tf_op jit(solution)/shard_map/reduce_scatter | solution.py:49
  199.5 2.0 fusion.21
  201.6 74.7 %all-gather.6.cloned.1.call-done = bf16[4096,512]{1,0:T(8,128)(2,1)} async-done(((bf16[256,512]{1,0:T(8,128)(2,1)}), bf16[4096,512]{1,0:T(8,128)(2,1)}) %all-gather.6.cloned.1.call-update) | async-done | bytes 4194320 | tf_op jit(solution)/shard_map/all_gather | solution.py:54
  276.3 4.9 gather_fusion.1
  281.2 7.1 %multiply_bitcast_fusion = f32[32,128,512]{1,2,0:T(8,128)} fusion(f32[32]{0:T(128)S(1)} %get-tuple-element.53, bf16[32,128,512]{2,1,0:T(8,128)(2,1)} %gather_fusion.1, pred[32]{0:T(512)(128)(4,1)S(1)} %compare_and_fusion, bf16[1,1,32,128,128]{4,3,2,1,0:T(8,128)(2,1)S(1)} %copy-done), kind=kOutput, calls=%fused_computation.4 | convolution fusion | flops 541065216 | bytes 13631648 | tf_op jit(solution)/shard_map/while/body/eval_jaxpr/kba,kbf->kaf/dot_general | solution.py:18
  288.4 9.0 %copy.21 = f32[32,128,512]{2,1,0:T(8,128)} copy(f32[32,128,512]{1,2,0:T(8,128)} %multiply_bitcast_fusion) | data formatting | bytes 16777216 | tf_op jit(solution)/shard_map/while/body/eval_jaxpr/mul | solution.py:22
  297.4 4.3 broadcast.55
  301.7 18.9 %scatter_fusion.1 = f32[32,128,512]{2,1,0:T(8,128)} fusion(f32[32,128,512]{2,1,0:T(8,128)} %broadcast.55, s32[32]{0:T(128)S(1)} %fusion.23, f32[32,128,512]{2,1,0:T(8,128)} %copy.21), kind=kCustom, calls=%fused_computation.3 | custom fusion | flops 2097152 | bytes 25165952 | tf_op jit(solution)/shard_map/while/body/eval_jaxpr/scatter-add | solution.py:22
  320.6 6.0 convert_element_type.48
  326.7 67.3 %reduce-scatter.8.cloned.1.call-done = bf16[256,512]{1,0:T(8,128)(2,1)} async-done(((bf16[4096,512]{1,0:T(8,128)(2,1)}), bf16[256,512]{1,0:T(8,128)(2,1)}) %reduce-scatter.8.cloned.1.call-update) | async-done | bytes 262160 | tf_op jit(solution)/shard_map/reduce_scatter | solution.py:58
  396.7 63.2 %reduce-scatter.10.cloned.1.call-done = f32[32,512]{1,0:T(8,128)} async-done(((f32[512,512]{1,0:T(8,128)}), f32[32,512]{1,0:T(8,128)}) %reduce-scatter.10.cloned.1.call-update) | async-done | bytes 65552
  459.9 1.7 copy.26
  461.7 157.9 %all-reduce.2.cloned.1.call-done = f32[32,512]{0,1:T(8,128)} async-done(((f32[32,512]{0,1:T(8,128)}), f32[32,512]{0,1:T(8,128)}) %all-reduce.2.cloned.1.call-update) | async-done | bytes 65552 | tf_op jit(solution)/shard_map/psum | solution.py:65
  619.6 1.7 copy.22
  622.4 43.7 %all-gather.8.cloned.1.call-done = f32[512,512]{1,0:T(8,128)} async-done(((f32[32,512]{1,0:T(8,128)}), f32[512,512]{1,0:T(8,128)}) %all-gather.8.cloned.1.call-update) | async-done | bytes 1048592 | tf_op jit(solution)/shard_map/all_gather | solution.py:66
  666.1 2.3 copy.32
  (41 shorter events, 6.1 us)
Async XLA Ops:
  7.2 52.2 %copy-start = (bf16[1,1,32,128,128]{4,3,2,1,0:T(8,128)(2,1)S(1)}, bf16[1,1,32,128,128]{4,3,2,1,0:T(8,128)(2,1)}, u32[]{:S(2)}) copy-start(bf16[1,1,32,128,128]{4,3,2,1,0:T(8,128)(2,1)} %param.11) | copy-start | bytes 3145732
  7.2 47.2 %all-gather.4.cloned.1.call-start = ((), (), s32[]{:S(2)}) async-start(), calls=%async_computation.3 | async-start | bytes 4456448 | tf_op jit(solution)/shard_map/all_gather | solution.py:45
  9.5 190.0 %reduce-scatter.6.cloned.1.call-start = ((), (), s32[]{:S(2)}) async-start(), calls=%async_computation.4 | async-start | bytes 4456448 | tf_op jit(solution)/shard_map/reduce_scatter | solution.py:49
  104.2 95.2 %copy-start.5 = (bf16[256,512]{1,0:T(8,128)(2,1)S(1)}, bf16[256,512]{1,0:T(8,128)(2,1)}, u32[]{:S(2)}) copy-start(bf16[256,512]{1,0:T(8,128)(2,1)} %param.15) | copy-start | bytes 786436
  104.3 97.3 %copy-start.7 = (s32[1,1,32]{2,1,0:T(1,128)S(1)}, s32[1,1,32]{2,1,0:T(1,128)}, u32[]{:S(2)}) copy-start(s32[1,1,32]{2,1,0:T(1,128)} %param.12) | copy-start | bytes 388
  104.3 97.3 %copy-start.6 = (s32[1,1,32]{2,1,0:T(1,128)S(1)}, s32[1,1,32]{2,1,0:T(1,128)}, u32[]{:S(2)}) copy-start(s32[1,1,32]{2,1,0:T(1,128)} %param.13) | copy-start | bytes 388
  104.3 172.0 %all-gather.6.cloned.1.call-start = ((), (), s32[]{:S(2)}) async-start(), calls=%async_computation.5 | async-start | bytes 4456448 | tf_op jit(solution)/shard_map/all_gather | solution.py:54
  201.5 192.5 %reduce-scatter.8.cloned.1.call-start = ((), (), s32[]{:S(2)}) async-start(), calls=%async_computation.6 | async-start | bytes 4456448 | tf_op jit(solution)/shard_map/reduce_scatter | solution.py:58
  326.6 67.4 %copy-start.3 = (bf16[256,512]{1,0:T(8,128)(2,1)S(1)}, bf16[256,512]{1,0:T(8,128)(2,1)}, u32[]{:S(2)}) copy-start(bf16[256,512]{1,0:T(8,128)(2,1)} %param.9) | copy-start | bytes 786436
  326.6 294.7 %copy-start.2 = (bf16[512,512]{1,0:T(8,128)(2,1)S(1)}, bf16[512,512]{1,0:T(8,128)(2,1)}, u32[]{:S(2)}) copy-start(bf16[512,512]{1,0:T(8,128)(2,1)} %param.10) | copy-start | bytes 1572868
  326.6 341.8 %copy-start.1 = (bf16[1,1,32,128,128]{4,3,2,1,0:T(8,128)(2,1)S(1)}, bf16[1,1,32,128,128]{4,3,2,1,0:T(8,128)(2,1)}, u32[]{:S(2)}) copy-start(bf16[1,1,32,128,128]{4,3,2,1,0:T(8,128)(2,1)} %param.11) | copy-start | bytes 3145732
  326.6 133.3 %reduce-scatter.10.cloned.1.call-start = ((), (), s32[]{:S(2)}) async-start(), calls=%async_computation.9 | async-start | bytes 1114112
  394.0 227.3 %copy-start.4 = (bf16[256,512]{1,0:T(8,128)(2,1)S(1)}, bf16[256,512]{1,0:T(8,128)(2,1)}, u32[]{:S(2)}) copy-start(bf16[256,512]{1,0:T(8,128)(2,1)} %reduce-scatter.8.cloned.1.call-done) | copy-start | bytes 786436
  396.7 222.9 %all-reduce.2.cloned.1.call-start = ((), (), s32[]{:S(2)}) async-start(), calls=%async_computation.7 | async-start | bytes 524288 | tf_op jit(solution)/shard_map/psum | solution.py:65
  461.6 204.5 %all-gather.8.cloned.1.call-start = ((), (), s32[]{:S(2)}) async-start(), calls=%async_computation.8 | async-start | bytes 1114112 | tf_op jit(solution)/shard_map/all_gather | solution.py:66
Sparse Core Ops, SparseCore 0:
  10.4 43.9 all-gather.3
  104.4 95.0 reduce-scatter.5
  202.5 73.7 all-gather.5
  326.7 67.2 reduce-scatter.7
  396.9 62.9 reduce-scatter.9
  463.0 156.5 all-reduce.1
  622.0 44.0 all-gather.7
where the time goes:
time: 676 us; the launch traced here: 675 us
  waiting for transfers between devices  544 us (80%)
  other arithmetic  53.3 us (8%)
  local copies, waits for them, and re-layouts  43.5 us (6%)
  matrix products  18.9 us (3%)
  between operations  14.9 us (2%)
    psum x1, waiting for transfers between devices, shards(): weight_part = lax.psum(weight_part, 'col')  158 us
    reduce_scatter x1, waiting for transfers between devices, shards(): lax.psum_scatter(forward_terms.astype(jnp.bfloat16), 'col', scatter_dimen...  95.2 us
    all_gather x1, waiting for transfers between devices, shards(): upstream = lax.all_gather(own_upstream, 'col', axis=0, tiled=True)  74.7 us
    reduce_scatter x1, waiting for transfers between devices, shards(): lax.psum_scatter(backward_terms.astype(jnp.bfloat16), 'row', scatter_dime...  67.3 us
    unnamed x8, waiting for transfers between devices  63.3 us
    all_gather x1, waiting for transfers between devices, shards(): grad_weight = lax.all_gather(weight_part, 'row', axis=0, tiled=True)  43.7 us
    all_gather x1, waiting for transfers between devices, shards(): panel = lax.all_gather(projected, 'row', axis=0, tiled=True)  42.2 us
    scatter-add x2, other arithmetic, one_group(): return running.at[target_ids].add(products * alive_mask[:, None, None])  37.4 us
  transfers between devices with their start and end apart: 7, of which 7 were waited for; matrix products, arithmetic and copies ran while one was open for 0% of the time, Pallas kernels for 0%

commit v1 on v0

--- a/solution.py
+++ b/solution.py
@@ -62,7 +62,7 @@
         features, grad_projected, (((0,), (0,)), ((), ())), preferred_element_type=jnp.float32
     )
     weight_part = lax.psum_scatter(weight_term, "row", scatter_dimension=0, tiled=True)
-    weight_part = lax.psum(weight_part, "col")
+    weight_part = jnp.sum(lax.all_gather(weight_part, "col"), axis=0)
     grad_weight = lax.all_gather(weight_part, "row", axis=0, tiled=True)
     grad_features = lax.dot_general(
         grad_projected, weight, (((1,), (1,)), ((), ())), preferred_element_type=jnp.float32

time: 676 us -> 562 us (0.83)
  waiting for transfers between devices: 544 us -> 431 us
    psum x1 -> x0, waiting for transfers between devices: 158 us -> none  [shards(): weight_part = lax.psum(weight_part, 'col')]
    reduce_scatter x0 -> x1, waiting for transfers between devices: none -> 63.2 us  [shards(): lax.psum_scatter(weight_term, 'row', scatter_dimension=0, tiled=True)]
    unnamed x8 -> x7, waiting for transfers between devices: 63.3 us -> 0.11 us
    all_gather x0 -> x1, waiting for transfers between devices: none -> 55.4 us  [shards(): weight_part = jnp.sum(lax.all_gather(weight_part, 'col'), axis=0)]
    all_gather x1, waiting for transfers between devices: 43.7 us -> 33.2 us  [shards(): grad_weight = lax.all_gather(weight_part, 'row', axis=0, tiled=True)]
  transfers between devices with their start and end apart: 7 -> 7, of which waited for: 7 -> 7; matrix products, arithmetic and copies ran while one was open for 0% -> 1% of each run, Pallas kernels for 0% -> 0%
where the time goes in v1:
time: 562 us; the launch traced here: 561 us
  waiting for transfers between devices  431 us (77%)
  other arithmetic  55.3 us (10%)
  local copies, waits for them, and re-layouts  40.2 us (7%)
  matrix products  18.9 us (3%)
  between operations  14.9 us (3%)
    reduce_scatter x1, waiting for transfers between devices, shards(): lax.psum_scatter(forward_terms.astype(jnp.bfloat16), 'col', scatter_dimen...  95.2 us
    all_gather x1, waiting for transfers between devices, shards(): upstream = lax.all_gather(own_upstream, 'col', axis=0, tiled=True)  74.7 us
    reduce_scatter x1, waiting for transfers between devices, shards(): lax.psum_scatter(backward_terms.astype(jnp.bfloat16), 'row', scatter_dime...  67.3 us
    reduce_scatter x1, waiting for transfers between devices, shards(): lax.psum_scatter(weight_term, 'row', scatter_dimension=0, tiled=True)  63.2 us
    all_gather x1, waiting for transfers between devices, shards(): weight_part = jnp.sum(lax.all_gather(weight_part, 'col'), axis=0)  55.4 us
    all_gather x1, waiting for transfers between devices, shards(): panel = lax.all_gather(projected, 'row', axis=0, tiled=True)  42.2 us
    scatter-add x2, other arithmetic, one_group(): return running.at[target_ids].add(products * alive_mask[:, None, None])  37.4 us
    all_gather x1, waiting for transfers between devices, shards(): grad_weight = lax.all_gather(weight_part, 'row', axis=0, tiled=True)  33.2 us
  transfers between devices with their start and end apart: 7, of which 7 were waited for; matrix products, arithmetic and copies ran while one was open for 1% of the time, Pallas kernels for 0%

profile of v1, /device:TPU:1, one launch (start us, length us, event | category | flops | bytes accessed | tf_op | source)
XLA Modules:
  0.0 560.7 jit_solution(14323665707563569961)
XLA Ops:
  7.2 2.2 convolution_convert_fusion.1
  12.1 42.2 %all-gather.6.cloned.1.call-done = bf16[4096,512]{1,0:T(8,128)(2,1)} async-done(((bf16[256,512]{1,0:T(8,128)(2,1)}), bf16[4096,512]{1,0:T(8,128)(2,1)}) %all-gather.6.cloned.1.call-update) | async-done | bytes 4194320 | tf_op jit(solution)/shard_map/all_gather | solution.py:45
  54.4 4.9 gather_fusion
  59.3 7.1 %multiply_bitcast_fusion.1 = f32[32,128,512]{1,2,0:T(8,128)} fusion(f32[32]{0:T(128)S(1)} %get-tuple-element.39, bf16[32,128,512]{2,1,0:T(8,128)(2,1)} %gather_fusion, pred[32]{0:T(512)(128)(4,1)S(1)} %get-tuple-element.38, bf16[1,1,32,128,128]{4,3,2,1,0:T(8,128)(2,1)S(1)} %copy-done), kind=kOutput, calls=%fused_computation.5 | convolution fusion | flops 541065216 | bytes 13631648 | tf_op jit(solution)/shard_map/while/body/eval_jaxpr/kab,kbf->kaf/dot_general | solution.py:20
  66.5 9.0 %copy.18 = f32[32,128,512]{2,1,0:T(8,128)} copy(f32[32,128,512]{1,2,0:T(8,128)} %multiply_bitcast_fusion.1) | data formatting | bytes 16777216 | tf_op jit(solution)/shard_map/while/body/eval_jaxpr/mul | solution.py:22
  75.5 4.3 broadcast.55.clone
  79.8 18.5 %scatter_fusion = f32[32,128,512]{2,1,0:T(8,128)} fusion(f32[32,128,512]{2,1,0:T(8,128)} %broadcast.55.clone, s32[32]{0:T(128)S(1)} %fusion.22, f32[32,128,512]{2,1,0:T(8,128)} %copy.18), kind=kCustom, calls=%fused_computation.2 | custom fusion | flops 2097152 | bytes 25165952 | tf_op jit(solution)/shard_map/while/body/eval_jaxpr/scatter-add | solution.py:22
  98.3 6.0 %convert_element_type.42 = bf16[32,128,512]{2,1,0:T(8,128)(2,1)} convert(f32[32,128,512]{2,1,0:T(8,128)} %scatter_fusion) | non-fusion elementwise | flops 2097152 | bytes 12582912 | tf_op jit(solution)/shard_map/convert_element_type | solution.py:50
  104.3 95.2 %reduce-scatter.6.cloned.1.call-done = bf16[256,512]{1,0:T(8,128)(2,1)} async-done(((bf16[4096,512]{1,0:T(8,128)(2,1)}), bf16[256,512]{1,0:T(8,128)(2,1)}) %reduce-scatter.6.cloned.1.call-update) | async-done | bytes 262160 | tf_op jit(solution)/shard_map/reduce_scatter | solution.py:49
  199.5 2.0 fusion.21
  201.6 74.7 %all-gather.8.cloned.1.call-done = bf16[4096,512]{1,0:T(8,128)(2,1)} async-done(((bf16[256,512]{1,0:T(8,128)(2,1)}), bf16[4096,512]{1,0:T(8,128)(2,1)}) %all-gather.8.cloned.1.call-update) | async-done | bytes 4194320 | tf_op jit(solution)/shard_map/all_gather | solution.py:54
  276.3 4.9 gather_fusion.1
  281.2 7.1 %multiply_bitcast_fusion = f32[32,128,512]{1,2,0:T(8,128)} fusion(f32[32]{0:T(128)S(1)} %get-tuple-element.39, bf16[32,128,512]{2,1,0:T(8,128)(2,1)} %gather_fusion.1, pred[32]{0:T(512)(128)(4,1)S(1)} %compare_and_fusion, bf16[1,1,32,128,128]{4,3,2,1,0:T(8,128)(2,1)S(1)} %copy-done), kind=kOutput, calls=%fused_computation.4 | convolution fusion | flops 541065216 | bytes 13631648 | tf_op jit(solution)/shard_map/while/body/eval_jaxpr/kba,kbf->kaf/dot_general | solution.py:18
  288.4 9.0 %copy.20 = f32[32,128,512]{2,1,0:T(8,128)} copy(f32[32,128,512]{1,2,0:T(8,128)} %multiply_bitcast_fusion) | data formatting | bytes 16777216 | tf_op jit(solution)/shard_map/while/body/eval_jaxpr/mul | solution.py:22
  297.4 4.3 broadcast.55
  301.7 18.9 %scatter_fusion.1 = f32[32,128,512]{2,1,0:T(8,128)} fusion(f32[32,128,512]{2,1,0:T(8,128)} %broadcast.55, s32[32]{0:T(128)S(1)} %fusion.23, f32[32,128,512]{2,1,0:T(8,128)} %copy.20), kind=kCustom, calls=%fused_computation.3 | custom fusion | flops 2097152 | bytes 25165952 | tf_op jit(solution)/shard_map/while/body/eval_jaxpr/scatter-add | solution.py:22
  320.6 6.0 %convert_element_type.48 = bf16[32,128,512]{2,1,0:T(8,128)(2,1)} convert(f32[32,128,512]{2,1,0:T(8,128)} %scatter_fusion.1) | non-fusion elementwise | flops 2097152 | bytes 12582912 | tf_op jit(solution)/shard_map/convert_element_type | solution.py:59
  326.7 67.3 %reduce-scatter.8.cloned.1.call-done = bf16[256,512]{1,0:T(8,128)(2,1)} async-done(((bf16[4096,512]{1,0:T(8,128)(2,1)}), bf16[256,512]{1,0:T(8,128)(2,1)}) %reduce-scatter.8.cloned.1.call-update) | async-done | bytes 262160 | tf_op jit(solution)/shard_map/reduce_scatter | solution.py:58
  394.0 1.3 convolution_bitcast_fusion
  396.7 63.2 %reduce-scatter.10.cloned.1.call-done = f32[32,512]{1,0:T(8,128)} async-done(((f32[512,512]{1,0:T(8,128)}), f32[32,512]{1,0:T(8,128)}) %reduce-scatter.10.cloned.1.call-update) | async-done | bytes 65552 | tf_op jit(solution)/shard_map/reduce_scatter | solution.py:64
  460.0 55.4 %all-gather.12.cloned.1.call-done = f32[512,512]{1,0:T(8,128)} async-done(((f32[32,512]{1,0:T(8,128)}), f32[512,512]{1,0:T(8,128)}) %all-gather.12.cloned.1.call-update) | async-done | bytes 1048592 | tf_op jit(solution)/shard_map/all_gather | solution.py:65
  515.4 1.9 reduce_sum.9
  518.4 33.2 %all-gather.10.cloned.1.call-done = f32[512,512]{1,0:T(8,128)} async-done(((f32[32,512]{1,0:T(8,128)}), f32[512,512]{1,0:T(8,128)}) %all-gather.10.cloned.1.call-update) | async-done | bytes 1048592 | tf_op jit(solution)/shard_map/all_gather | solution.py:66
  551.6 2.3 copy.31
  (40 shorter events, 4.8 us)
Async XLA Ops:
  7.2 52.2 %copy-start = (bf16[1,1,32,128,128]{4,3,2,1,0:T(8,128)(2,1)S(1)}, bf16[1,1,32,128,128]{4,3,2,1,0:T(8,128)(2,1)}, u32[]{:S(2)}) copy-start(bf16[1,1,32,128,128]{4,3,2,1,0:T(8,128)(2,1)} %param.11) | copy-start | bytes 3145732
  7.2 47.2 %all-gather.6.cloned.1.call-start = ((), (), s32[]{:S(2)}) async-start(), calls=%async_computation.3 | async-start | bytes 4456448 | tf_op jit(solution)/shard_map/all_gather | solution.py:45
  9.5 190.0 %reduce-scatter.6.cloned.1.call-start = ((), (), s32[]{:S(2)}) async-start(), calls=%async_computation.4 | async-start | bytes 4456448 | tf_op jit(solution)/shard_map/reduce_scatter | solution.py:49
  104.2 95.2 %copy-start.5 = (bf16[256,512]{1,0:T(8,128)(2,1)S(1)}, bf16[256,512]{1,0:T(8,128)(2,1)}, u32[]{:S(2)}) copy-start(bf16[256,512]{1,0:T(8,128)(2,1)} %param.15) | copy-start | bytes 786436
  104.3 97.3 %copy-start.7 = (s32[1,1,32]{2,1,0:T(1,128)S(1)}, s32[1,1,32]{2,1,0:T(1,128)}, u32[]{:S(2)}) copy-start(s32[1,1,32]{2,1,0:T(1,128)} %param.12) | copy-start | bytes 388
  104.3 97.3 %copy-start.6 = (s32[1,1,32]{2,1,0:T(1,128)S(1)}, s32[1,1,32]{2,1,0:T(1,128)}, u32[]{:S(2)}) copy-start(s32[1,1,32]{2,1,0:T(1,128)} %param.13) | copy-start | bytes 388
  104.3 172.0 %all-gather.8.cloned.1.call-start = ((), (), s32[]{:S(2)}) async-start(), calls=%async_computation.5 | async-start | bytes 4456448 | tf_op jit(solution)/shard_map/all_gather | solution.py:54
  201.5 192.5 %reduce-scatter.8.cloned.1.call-start = ((), (), s32[]{:S(2)}) async-start(), calls=%async_computation.6 | async-start | bytes 4456448 | tf_op jit(solution)/shard_map/reduce_scatter | solution.py:58
  326.6 67.4 %copy-start.3 = (bf16[256,512]{1,0:T(8,128)(2,1)S(1)}, bf16[256,512]{1,0:T(8,128)(2,1)}, u32[]{:S(2)}) copy-start(bf16[256,512]{1,0:T(8,128)(2,1)} %param.9) | copy-start | bytes 786436
  326.6 190.7 %copy-start.2 = (bf16[512,512]{1,0:T(8,128)(2,1)S(1)}, bf16[512,512]{1,0:T(8,128)(2,1)}, u32[]{:S(2)}) copy-start(bf16[512,512]{1,0:T(8,128)(2,1)} %param.10) | copy-start | bytes 1572868
  326.6 227.2 %copy-start.1 = (bf16[1,1,32,128,128]{4,3,2,1,0:T(8,128)(2,1)S(1)}, bf16[1,1,32,128,128]{4,3,2,1,0:T(8,128)(2,1)}, u32[]{:S(2)}) copy-start(bf16[1,1,32,128,128]{4,3,2,1,0:T(8,128)(2,1)} %param.11) | copy-start | bytes 3145732
  326.6 133.3 %reduce-scatter.10.cloned.1.call-start = ((), (), s32[]{:S(2)}) async-start(), calls=%async_computation.9 | async-start | bytes 1114112 | tf_op jit(solution)/shard_map/reduce_scatter | solution.py:64
  394.0 123.3 %copy-start.4 = (bf16[256,512]{1,0:T(8,128)(2,1)S(1)}, bf16[256,512]{1,0:T(8,128)(2,1)}, u32[]{:S(2)}) copy-start(bf16[256,512]{1,0:T(8,128)(2,1)} %reduce-scatter.8.cloned.1.call-done) | copy-start | bytes 786436
  396.7 118.7 %all-gather.12.cloned.1.call-start = ((), (), s32[]{:S(2)}) async-start(), calls=%async_computation.8 | async-start | bytes 1114112 | tf_op jit(solution)/shard_map/all_gather | solution.py:65
  460.0 91.6 %all-gather.10.cloned.1.call-start = ((), (), s32[]{:S(2)}) async-start(), calls=%async_computation.7 | async-start | bytes 1114112 | tf_op jit(solution)/shard_map/all_gather | solution.py:66
Sparse Core Ops, SparseCore 0:
  10.4 43.9 all-gather.5
  104.4 95.0 reduce-scatter.5
  202.5 73.7 all-gather.7
  326.7 67.2 reduce-scatter.7
  396.9 62.9 reduce-scatter.9
  462.2 53.1 all-gather.11
  517.8 33.7 all-gather.9
